TPU v7x, 256 devices: a whole 4x4x8 slice. The times are simulated.
256 devices in a mesh: section: 8 (over z), ctx: 32 (over x, y, core).
Axes of the slice: x: 4, y: 4, z: 8, core: 2. Of those that a mesh axis runs over, the one named last changes fastest.
Arguments:
- query_rows: bfloat16 [8, 8192, 2048], P('section', 'ctx'), may hold values from -40 to 40
- key_rows: bfloat16 [8, 8192, 1024], P('section', 'ctx'), may hold values from -6 to 6
- value_rows: bfloat16 [8, 8192, 1024], P('section', 'ctx'), may hold values from -6 to 6
- finished_grad: bfloat16 [8, 8192, 2048], P('section', 'ctx'), may hold values from -96 to 96
- doc_lengths: int32 [4], replicated, may hold values from 1 to 4096, as said below
Outputs:
- query_grad: bfloat16 [8, 8192, 2048], P('section', 'ctx')
- key_grad: bfloat16 [8, 8192, 1024], P('section', 'ctx')
- value_grad: bfloat16 [8, 8192, 1024], P('section', 'ctx')
Inputs may be any that keep to these rules, and one draw needn't show every extreme that they name: `doc_lengths`: document lengths add up to 8192; the longest is exactly 4096.
All inputs are finite; a program needn't handle non-finite values.
Results may differ from a plain program's by a relative error of at most 0.04.
Values may be sent and summed in bfloat16 or wider, within the bound.
No kernel may reach another device: no remote copies, remote signals or barrier semaphores. Data moves between devices by JAX's collectives and lax.ppermute only.
A program may use at most 128 MiB of HBM per device.

v0:
```python
import jax
import jax.numpy as jnp
from jax import lax
from jax.experimental import pallas as pl
from jax.experimental.pallas import tpu as pltpu
from jax.sharding import PartitionSpec as P


WINDOW = 1024
KV_HEADS = 8
CHUNK_GROUPS = (5, 3)
GROUP = 2


SCORE_SCALE = 168.0 ** (-0.5)


def product(a, b, dims):
    return lax.dot_general(a, b, dims, preferred_element_type=jnp.float32)


def attention_back_kernel(at_ref, q_ref, do_ref, *refs):
    blocks = len(refs) - 4
    piece_refs = refs[:blocks]
    mask_ref = refs[blocks]
    dq_ref, far_ref, own_ref = refs[-3:]
    head_size = piece_refs[0].shape[2]
    heads = q_ref.shape[1] // head_size
    rows = q_ref.shape[0]
    allowed = mask_ref[...] > 0
    keys = jnp.concatenate([ref[0] for ref in piece_refs], axis=0)
    values = jnp.concatenate([ref[1] for ref in piece_refs], axis=0)
    queries = jnp.concatenate([q_ref[:, h * head_size:(h + 1) * head_size] for h in range(heads)], axis=0)
    grads = jnp.concatenate([do_ref[:, h * head_size:(h + 1) * head_size] for h in range(heads)], axis=0)
    allowed = jnp.concatenate([allowed] * heads, axis=0)
    nt = (((1,), (1,)), ((), ()))
    nn = (((1,), (0,)), ((), ()))
    scores = SCORE_SCALE * product(queries, keys, nt)
    scores = jnp.where(allowed, scores, -jnp.inf)
    highest = jnp.max(scores, axis=-1, keepdims=True)
    shifted_exp = jnp.exp(scores - highest)
    weights = shifted_exp * (1.0 / jnp.sum(shifted_exp, axis=-1, keepdims=True))
    weight_half = weights.astype(jnp.bfloat16)
    attended = product(weight_half, values, nn).astype(jnp.bfloat16)
    row_dot = jnp.sum(attended.astype(jnp.float32) * grads.astype(jnp.float32), axis=-1, keepdims=True)
    weight_grad = product(grads, values, nt)
    score_grad = (weights * (weight_grad - row_dot)).astype(jnp.bfloat16)
    query_back = SCORE_SCALE * product(score_grad, keys, nn)
    for h in range(heads):
        dq_ref[:, h * head_size:(h + 1) * head_size] = query_back[h * rows:(h + 1) * rows].astype(dq_ref.dtype)
    key_back = (SCORE_SCALE * product(queries.T, score_grad, nn)).T
    value_back = product(grads.T, weight_half, nn).T
    for block in range(blocks - 1):
        lines = slice(block * rows, (block + 1) * rows)
        far_ref[block, 0] = key_back[lines].astype(far_ref.dtype)
        far_ref[block, 1] = value_back[lines].astype(far_ref.dtype)
    own_ref[0] = key_back[(blocks - 1) * rows:]
    own_ref[1] = value_back[(blocks - 1) * rows:]


def attention_back(queries, grads, window_pieces, allowed, query_group, kv_group, groups):
    rows, width = queries.shape
    head_size = width // (GROUP * KV_HEADS)
    group_width = GROUP * head_size
    span = rows * len(window_pieces)
    q_spec = pl.BlockSpec((rows, group_width), lambda g, at: (0, g + at[0]))
    piece_spec = pl.BlockSpec((2, rows, head_size), lambda g, at: (0, 0, g + at[1]))
    mask_spec = pl.BlockSpec((rows, span), lambda g, at: (0, 0))
    far_spec = pl.BlockSpec((len(window_pieces) - 1, 2, rows, head_size), lambda g, at: (0, 0, 0, g))
    own_spec = pl.BlockSpec((2, rows, head_size), lambda g, at: (0, 0, g))
    inputs = [queries, grads, *window_pieces, allowed]
    dq_spec = pl.BlockSpec((rows, group_width), lambda g, at: (0, g))
    grid_spec = pltpu.PrefetchScalarGridSpec(
        num_scalar_prefetch=1,
        grid=(groups,),
        in_specs=[q_spec, q_spec] + [piece_spec] * len(window_pieces) + [mask_spec],
        out_specs=[dq_spec, far_spec, own_spec],
    )
    chunk_width = groups * head_size
    return pl.pallas_call(
        attention_back_kernel,
        grid_spec=grid_spec,
        out_shape=[
            jax.ShapeDtypeStruct((rows, groups * group_width), jnp.bfloat16),
            jax.ShapeDtypeStruct((len(window_pieces) - 1, 2, rows, chunk_width), jnp.bfloat16),
            jax.ShapeDtypeStruct((2, rows, chunk_width), jnp.float32),
        ],
        compiler_params=pltpu.CompilerParams(vmem_limit_bytes=60 * 1024 * 1024),
    )(jnp.array([query_group, kv_group], jnp.int32), *inputs)


def passed_along(shard, axis, by):
    count = lax.axis_size(axis)
    return lax.ppermute(shard, axis, [(i, (i + by) % count) for i in range(count)])


def shifted(value, axis, steps):
    count = lax.axis_size(axis)
    initial, last = (max(0, -steps), min(count, count - steps))
    return lax.ppermute(value, axis, [(source, source + steps) for source in range(initial, last)])


def doc_number(positions, doc_lengths):
    ends = jnp.cumsum(doc_lengths)
    return jnp.sum((positions[:, None] >= ends[None, :]).astype(jnp.int32), axis=1)


def window_mask(query_pos, key_pos, doc_lengths):
    same_doc = (
        doc_number(query_pos, doc_lengths)[:, None] == doc_number(key_pos, doc_lengths)[None, :]
    )
    spacing = query_pos[:, None] - key_pos[None, :]
    return same_doc & (spacing >= 0) & (spacing < WINDOW) & (key_pos[None, :] >= 0)


def local_body(query_rows, key_rows, value_rows, finished_grad, doc_lengths):
    queries = query_rows[0]
    keys_here = key_rows[0]
    values_here = value_rows[0]
    count_rows = queries.shape[0]
    pair_width = keys_here.shape[1]
    head_size = pair_width // KV_HEADS
    rank_here = lax.axis_index("ctx")
    first_pos = rank_here * count_rows
    arriving = passed_along(finished_grad, "section", -1)[0]
    query_pos = first_pos + jnp.arange(count_rows, dtype=jnp.int32)
    key_pos = first_pos - WINDOW + jnp.arange(WINDOW + count_rows, dtype=jnp.int32)
    allowed = window_mask(query_pos, key_pos, doc_lengths).astype(jnp.float32)
    mask = allowed.astype(jnp.bfloat16)

    odd = (rank_here % 2) == 1

    def partner(value):
        count = lax.axis_size("ctx")
        return lax.ppermute(value, "ctx", [(i, i ^ 1) for i in range(count)])

    def forward(own):
        minus_two = shifted(own, "ctx", 2)
        minus_one = partner(jnp.where(odd, minus_two, own))
        minus_four = shifted(minus_two, "ctx", 2)
        minus_three = partner(jnp.where(odd, minus_four, minus_two))
        return [minus_four, minus_three, minus_two, minus_one, own]

    def backward(far, own):
        passed = partner(jnp.stack([far[3], far[1]])).astype(jnp.float32)
        zero = jnp.zeros_like(passed[0])
        to_four = far[0].astype(jnp.float32) + jnp.where(odd, passed[1], zero)
        to_two = far[2].astype(jnp.float32) + jnp.where(odd, passed[0], passed[1])
        direct = jnp.where(odd, zero, passed[0])
        arrived = shifted(to_four.astype(jnp.bfloat16), "ctx", -2).astype(jnp.float32)
        arrived = shifted((arrived + to_two).astype(jnp.bfloat16), "ctx", -2).astype(jnp.float32)
        return (own + (arrived + direct)).astype(jnp.bfloat16)

    firsts = [sum(CHUNK_GROUPS[:chunk]) for chunk in range(len(CHUNK_GROUPS))]
    query_parts = []
    totals = []
    windows = []
    after = None
    for chunk, groups in enumerate(CHUNK_GROUPS):
        cols = slice(firsts[chunk] * head_size, (firsts[chunk] + groups) * head_size)
        own_pair = jnp.stack([keys_here[:, cols], values_here[:, cols]])
        if after is not None:
            own_pair = lax.optimization_barrier((own_pair, after))[0]
        windows.append(forward(own_pair))
        after = windows[-1][0]
    for chunk, groups in enumerate(CHUNK_GROUPS):
        query_part, far, own = attention_back(
            queries, arriving, windows[chunk], mask, firsts[chunk], 0, groups
        )
        query_parts.append(query_part)
        totals.append(backward(far, own))
    query_back = jnp.concatenate(query_parts, axis=1)

    return (
        query_back[None],
        jnp.concatenate([total[0] for total in totals], axis=1)[None],
        jnp.concatenate([total[1] for total in totals], axis=1)[None],
    )


def solution(mesh):
    return jax.shard_map(
        local_body,
        mesh=mesh,
        in_specs=(
            P("section", "ctx", None),
            P("section", "ctx", None),
            P("section", "ctx", None),
            P("section", "ctx", None),
            P(),
        ),
        out_specs=(P("section", "ctx", None), P("section", "ctx", None), P("section", "ctx", None)),
        check_vma=False,
    )
```

profile of v0, /device:TPU:25, one launch (start us, length us, event | category | flops | bytes accessed | tf_op | source)
XLA Modules:
  0.0 153.4 jit_solution(10245935109621681055)
XLA Ops:
  0.6 1.1 slice_bitcast_fusion.2
  1.8 0.1 pad_maximum_fusion.2.refs_4_
  1.9 2.8 %collective-permute-start.1 = (bf16[2,256,640]{2,1,0:T(8,128)(2,1)S(1)}, bf16[2,256,640]{2,1,0:T(8,128)(2,1)S(1)}, u32[]{:S(2)}, u32[]{:S(2)}) collective-permute-start(bf16[2,256,640]{2,1,0:T(8,128)(2,1)S(1)} %pad_maximum_fusion.2.refs_4_), channel_id=1, source_target_pairs={{0,2},{1,3},{2,4},{3,5},{4,6},{5,7},{6,8},{7,9},{8,10},{9,11},{10,... | collective-permute-start | bytes 1966088 | tf_op jit(solution)/shard_map/ppermute | solution.py:100
  4.7 5.7 %collective-permute-start = (bf16[1,256,2048]{2,1,0:T(8,128)(2,1)}, bf16[1,256,2048]{2,1,0:T(8,128)(2,1)S(1)}, u32[]{:S(2)}, u32[]{:S(2)}) collective-permute-start(bf16[1,256,2048]{2,1,0:T(8,128)(2,1)} %param.10), channel_id=1, source_target_pairs={{0,224},{32,0},{64,32},{96,64},{128,96},{160,128},{192,160},{224,1... | collective-permute-start | bytes 3145736 | tf_op jit(solution)/shard_map/ppermute | solution.py:94
  10.3 0.2 reduce-window.8
  10.5 8.9 %collective-permute-done.1.refs_2_ = bf16[2,256,640]{2,1,0:T(8,128)(2,1)S(1)} collective-permute-done((bf16[2,256,640]{2,1,0:T(8,128)(2,1)S(1)}, bf16[2,256,640]{2,1,0:T(8,128)(2,1)S(1)}, u32[]{:S(2)}, u32[]{:S(2)}) %collective-permute-start.1) | collective-permute-done | bytes 655392 | tf_op jit(solution)/shard_map/ppermute | solution.py:100
  19.4 4.9 %collective-permute-start.2 = (bf16[2,256,640]{2,1,0:T(8,128)(2,1)S(1)}, bf16[2,256,640]{2,1,0:T(8,128)(2,1)S(1)}, u32[]{:S(2)}, u32[]{:S(2)}) collective-permute-start(bf16[2,256,640]{2,1,0:T(8,128)(2,1)S(1)} %collective-permute-done.1.refs_2_), channel_id=1, source_target_pairs={{0,2},{1,3},{2,4},{3,5},{4,6},{5,7},{6,8},{7,9},{8,10},{9,11},{10,... | collective-permute-start | bytes 1966088 | tf_op jit(solution)/shard_map/ppermute | solution.py:100
  24.3 0.1 convert_reduce_fusion.1
  24.4 1.1 slice_bitcast_fusion.6
  25.5 11.3 %collective-permute-done.2.refs_0_ = bf16[2,256,640]{2,1,0:T(8,128)(2,1)S(1)} collective-permute-done((bf16[2,256,640]{2,1,0:T(8,128)(2,1)S(1)}, bf16[2,256,640]{2,1,0:T(8,128)(2,1)S(1)}, u32[]{:S(2)}, u32[]{:S(2)}) %collective-permute-start.2) | collective-permute-done | bytes 655392 | tf_op jit(solution)/shard_map/ppermute | solution.py:100
  36.8 6.2 %collective-permute-start.5 = (bf16[2,256,384]{2,1,0:T(8,128)(2,1)S(1)}, bf16[2,256,384]{2,1,0:T(8,128)(2,1)S(1)}, u32[]{:S(2)}, u32[]{:S(2)}) collective-permute-start(bf16[2,256,384]{2,1,0:T(8,128)(2,1)S(1)} %pad_maximum_fusion.3.refs_4_), channel_id=1, source_target_pairs={{0,2},{1,3},{2,4},{3,5},{4,6},{5,7},{6,8},{7,9},{8,10},{9,11},{10,... | collective-permute-start | bytes 1179656 | tf_op jit(solution)/shard_map/ppermute | solution.py:100
  43.0 0.1 broadcast_select_fusion
  43.2 2.8 %collective-permute-start.3 = (bf16[2,256,640]{2,1,0:T(8,128)(2,1)S(1)}, bf16[2,256,640]{2,1,0:T(8,128)(2,1)S(1)}, u32[]{:S(2)}, u32[]{:S(2)}) collective-permute-start(bf16[2,256,640]{2,1,0:T(8,128)(2,1)S(1)} %get-tuple-element.24), channel_id=1, source_target_pairs={{0,1},{1,0},{2,3},{3,2},{4,5},{5,4},{6,7},{7,6},{8,9},{9,8},{10,11... | collective-permute-start | bytes 1966088 | tf_op jit(solution)/shard_map/ppermute | solution.py:135
  46.0 0.1 collective-permute-start.4
  46.1 0.1 convert_reduce_fusion
  46.2 2.9 %collective-permute-done.5.refs_2_ = bf16[2,256,384]{2,1,0:T(8,128)(2,1)S(1)} collective-permute-done((bf16[2,256,384]{2,1,0:T(8,128)(2,1)S(1)}, bf16[2,256,384]{2,1,0:T(8,128)(2,1)S(1)}, u32[]{:S(2)}, u32[]{:S(2)}) %collective-permute-start.5) | collective-permute-done | bytes 393248 | tf_op jit(solution)/shard_map/ppermute | solution.py:100
  49.1 6.2 %collective-permute-start.6 = (bf16[2,256,384]{2,1,0:T(8,128)(2,1)S(1)}, bf16[2,256,384]{2,1,0:T(8,128)(2,1)S(1)}, u32[]{:S(2)}, u32[]{:S(2)}) collective-permute-start(bf16[2,256,384]{2,1,0:T(8,128)(2,1)S(1)} %collective-permute-done.5.refs_2_), channel_id=1, source_target_pairs={{0,2},{1,3},{2,4},{3,5},{4,6},{5,7},{6,8},{7,9},{8,10},{9,11},{10,... | collective-permute-start | bytes 1179656 | tf_op jit(solution)/shard_map/ppermute | solution.py:100
  55.3 1.4 convert_convert_fusion.refs_5_
  56.7 0.0 collective-permute-done
  56.7 0.0 collective-permute-done.3.refs_1_
  56.7 0.0 collective-permute-done.4.refs_3_
  56.7 0.6 call_exported.0.at_ref
  57.3 0.4 copy-done
  57.7 0.3 copy-done.11
  57.9 0.2 copy-done.12
  58.1 18.4 %shard_map.94 = (bf16[256,1280]{1,0:T(8,128)(2,1)}, bf16[4,2,256,640]{3,2,1,0:T(8,128)(2,1)}, f32[2,256,640]{2,1,0:T(8,128)}) custom-call(s32[2]{0:T(128)} %call_exported.0.at_ref, bf16[256,2048]{1,0:T(8,128)(2,1)} %bitcast.52, bf16[256,2048]{1,0:T(8,128)(2,1)} %bitcast.54, bf16[2,256,640]{2,1,0:T(8,128)(2,1)} %copy-done.5, bf16[2,256,640]{2,1,0:T(8,128)(2,1)} %copy-done.11, ...), custom_call_target="tpu_custom_call" | custom-call | tf_op jit(solution)/shard_map/pallas_call | solution.py:80
  76.5 0.0 collective-permute-done.6.refs_0_
  76.5 0.0 copy-start.7
  76.5 0.1 broadcast_select_fusion.2
  76.6 3.6 %collective-permute-start.7 = (bf16[2,256,384]{2,1,0:T(8,128)(2,1)S(1)}, bf16[2,256,384]{2,1,0:T(8,128)(2,1)S(1)}, u32[]{:S(2)}, u32[]{:S(2)}) collective-permute-start(bf16[2,256,384]{2,1,0:T(8,128)(2,1)S(1)} %get-tuple-element.28), channel_id=1, source_target_pairs={{0,1},{1,0},{2,3},{3,2},{4,5},{5,4},{6,7},{7,6},{8,9},{9,8},{10,11... | collective-permute-start | bytes 1179656 | tf_op jit(solution)/shard_map/ppermute | solution.py:135
  80.2 0.1 collective-permute-start.8
  80.3 1.4 fusion.11
  81.7 0.1 pad_maximum_fusion
  81.9 0.5 collective-permute-start.9
  82.4 0.0 collective-permute-done.7.refs_1_
  82.4 0.0 collective-permute-done.8.refs_3_
  82.4 0.7 copy-done.15
  83.1 0.8 copy-done.16
  83.9 12.2 %shard_map.95 = (bf16[256,768]{1,0:T(8,128)(2,1)}, bf16[4,2,256,384]{3,2,1,0:T(8,128)(2,1)}, f32[2,256,384]{2,1,0:T(8,128)}) custom-call(s32[2]{0:T(128)} %constant.40.clone.at_ref, bf16[256,2048]{1,0:T(8,128)(2,1)} %bitcast.53, bf16[256,2048]{1,0:T(8,128)(2,1)} %bitcast.55, bf16[2,256,384]{2,1,0:T(8,128)(2,1)} %copy-done.7, ...), custom_call_target="tpu_custom_call" | custom-call | tf_op jit(solution)/shard_map/pallas_call | solution.py:80
  96.1 1.2 fusion.12
  97.3 0.1 pad_maximum_fusion.1
  97.4 0.2 collective-permute-start.12
  97.6 2.2 %collective-permute-done.12 = bf16[2,2,256,384]{3,2,1,0:T(8,128)(2,1)S(1)} collective-permute-done((bf16[2,2,256,384]{3,2,1,0:T(8,128)(2,1)S(1)}, bf16[2,2,256,384]{3,2,1,0:T(8,128)(2,1)S(1)}, u32[]{:S(2)}, u32[]{:S(2)}) %collective-permute-start.12) | collective-permute-done | bytes 786464 | tf_op jit(solution)/shard_map/ppermute | solution.py:135
  99.8 0.1 convert_element_type.84
  99.9 0.1 fusion.10
  100.1 2.2 %collective-permute-start.13 = (bf16[2,256,384]{2,1,0:T(8,128)(2,1)S(1)}, bf16[2,256,384]{2,1,0:T(8,128)(2,1)S(1)}, u32[]{:S(2)}, u32[]{:S(2)}) collective-permute-start(bf16[2,256,384]{2,1,0:T(8,128)(2,1)S(1)} %fusion.10), channel_id=1, source_target_pairs={{2,0},{3,1},{4,2},{5,3},{6,4},{7,5},{8,6},{9,7},{10,8},{11,9},{12,... | collective-permute-start | bytes 1179656 | tf_op jit(solution)/shard_map/ppermute | solution.py:100
  102.3 0.0 collective-permute-done.9
  102.3 0.2 convert_element_type.75
  102.5 0.2 fusion.9
  102.6 1.9 %collective-permute-start.10 = (bf16[2,256,640]{2,1,0:T(8,128)(2,1)S(1)}, bf16[2,256,640]{2,1,0:T(8,128)(2,1)S(1)}, u32[]{:S(2)}, u32[]{:S(2)}) collective-permute-start(bf16[2,256,640]{2,1,0:T(8,128)(2,1)S(1)} %fusion.9), channel_id=1, source_target_pairs={{2,0},{3,1},{4,2},{5,3},{6,4},{7,5},{8,6},{9,7},{10,8},{11,9},{12,... | collective-permute-start | bytes 1966088 | tf_op jit(solution)/shard_map/ppermute | solution.py:100
  104.6 10.3 %collective-permute-done.13 = bf16[2,256,384]{2,1,0:T(8,128)(2,1)S(1)} collective-permute-done((bf16[2,256,384]{2,1,0:T(8,128)(2,1)S(1)}, bf16[2,256,384]{2,1,0:T(8,128)(2,1)S(1)}, u32[]{:S(2)}, u32[]{:S(2)}) %collective-permute-start.13) | collective-permute-done | bytes 393248 | tf_op jit(solution)/shard_map/ppermute | solution.py:100
  114.9 0.2 fusion.8
  115.1 2.1 %collective-permute-start.14 = (bf16[2,256,384]{2,1,0:T(8,128)(2,1)S(1)}, bf16[2,256,384]{2,1,0:T(8,128)(2,1)S(1)}, u32[]{:S(2)}, u32[]{:S(2)}) collective-permute-start(bf16[2,256,384]{2,1,0:T(8,128)(2,1)S(1)} %fusion.8), channel_id=1, source_target_pairs={{2,0},{3,1},{4,2},{5,3},{6,4},{7,5},{8,6},{9,7},{10,8},{11,9},{12,... | collective-permute-start | bytes 1179656 | tf_op jit(solution)/shard_map/ppermute | solution.py:100
  117.2 11.7 %collective-permute-done.10 = bf16[2,256,640]{2,1,0:T(8,128)(2,1)S(1)} collective-permute-done((bf16[2,256,640]{2,1,0:T(8,128)(2,1)S(1)}, bf16[2,256,640]{2,1,0:T(8,128)(2,1)S(1)}, u32[]{:S(2)}, u32[]{:S(2)}) %collective-permute-start.10) | collective-permute-done | bytes 655392 | tf_op jit(solution)/shard_map/ppermute | solution.py:100
  128.9 0.3 fusion.2
  129.2 2.1 %collective-permute-start.11 = (bf16[2,256,640]{2,1,0:T(8,128)(2,1)S(1)}, bf16[2,256,640]{2,1,0:T(8,128)(2,1)S(1)}, u32[]{:S(2)}, u32[]{:S(2)}) collective-permute-start(bf16[2,256,640]{2,1,0:T(8,128)(2,1)S(1)} %fusion.2), channel_id=1, source_target_pairs={{2,0},{3,1},{4,2},{5,3},{6,4},{7,5},{8,6},{9,7},{10,8},{11,9},{12,... | collective-permute-start | bytes 1966088 | tf_op jit(solution)/shard_map/ppermute | solution.py:100
  131.3 1.1 maximum_bitcast_fusion
  132.4 5.0 %collective-permute-done.14 = bf16[2,256,384]{2,1,0:T(8,128)(2,1)S(1)} collective-permute-done((bf16[2,256,384]{2,1,0:T(8,128)(2,1)S(1)}, bf16[2,256,384]{2,1,0:T(8,128)(2,1)S(1)}, u32[]{:S(2)}, u32[]{:S(2)}) %collective-permute-start.14) | collective-permute-done | bytes 393248 | tf_op jit(solution)/shard_map/ppermute | solution.py:100
  137.4 0.2 fusion.7
  137.6 13.8 %collective-permute-done.11 = bf16[2,256,640]{2,1,0:T(8,128)(2,1)S(1)} collective-permute-done((bf16[2,256,640]{2,1,0:T(8,128)(2,1)S(1)}, bf16[2,256,640]{2,1,0:T(8,128)(2,1)S(1)}, u32[]{:S(2)}, u32[]{:S(2)}) %collective-permute-start.11) | collective-permute-done | bytes 655392 | tf_op jit(solution)/shard_map/ppermute | solution.py:100
  151.4 0.2 fusion.1
  151.6 0.1 slice_bitcast_fusion
  151.7 0.9 maximum_bitcast_fusion.2
  152.5 0.9 maximum_bitcast_fusion.1
  (35 shorter events, 0.2 us)
Async XLA Ops:
  0.6 9.7 %copy-start.17 = (s32[4]{0:T(128)S(1)}, s32[4]{0:T(128)}, u32[]{:S(2)}) copy-start(s32[4]{0:T(128)} %param.11) | copy-start | bytes 52
  1.9 41.3 %copy-start.2 = (bf16[2,256,640]{2,1,0:T(8,128)(2,1)}, bf16[2,256,640]{2,1,0:T(8,128)(2,1)S(1)}, u32[]{:S(2)}) copy-start(bf16[2,256,640]{2,1,0:T(8,128)(2,1)S(1)} %pad_maximum_fusion.2.refs_4_) | copy-start | bytes 1966084
  1.9 17.5 %collective-permute-start.1 = (bf16[2,256,640]{2,1,0:T(8,128)(2,1)S(1)}, bf16[2,256,640]{2,1,0:T(8,128)(2,1)S(1)}, u32[]{:S(2)}, u32[]{:S(2)}) collective-permute-start(bf16[2,256,640]{2,1,0:T(8,128)(2,1)S(1)} %pad_maximum_fusion.2.refs_4_), channel_id=1, source_target_pairs={{0,2},{1,3},{2,4},{3,5},{4,6},{5,7},{6,8},{7,9},{8,10},{9,11},{10,... | collective-permute-start | bytes 1966088 | tf_op jit(solution)/shard_map/ppermute | solution.py:100
  4.7 52.0 %collective-permute-start = (bf16[1,256,2048]{2,1,0:T(8,128)(2,1)}, bf16[1,256,2048]{2,1,0:T(8,128)(2,1)S(1)}, u32[]{:S(2)}, u32[]{:S(2)}) collective-permute-start(bf16[1,256,2048]{2,1,0:T(8,128)(2,1)} %param.10), channel_id=1, source_target_pairs={{0,224},{32,0},{64,32},{96,64},{128,96},{160,128},{192,160},{224,1... | collective-permute-start | bytes 3145736 | tf_op jit(solution)/shard_map/ppermute | solution.py:94
  19.4 23.8 %copy-start.4 = (bf16[2,256,640]{2,1,0:T(8,128)(2,1)}, bf16[2,256,640]{2,1,0:T(8,128)(2,1)S(1)}, u32[]{:S(2)}) copy-start(bf16[2,256,640]{2,1,0:T(8,128)(2,1)S(1)} %collective-permute-done.1.refs_2_) | copy-start | bytes 1966084
  19.4 17.4 %collective-permute-start.2 = (bf16[2,256,640]{2,1,0:T(8,128)(2,1)S(1)}, bf16[2,256,640]{2,1,0:T(8,128)(2,1)S(1)}, u32[]{:S(2)}, u32[]{:S(2)}) collective-permute-start(bf16[2,256,640]{2,1,0:T(8,128)(2,1)S(1)} %collective-permute-done.1.refs_2_), channel_id=1, source_target_pairs={{0,2},{1,3},{2,4},{3,5},{4,6},{5,7},{6,8},{7,9},{8,10},{9,11},{10,... | collective-permute-start | bytes 1966088 | tf_op jit(solution)/shard_map/ppermute | solution.py:100
  25.5 51.0 %copy-start.1 = (bf16[2,256,384]{2,1,0:T(8,128)(2,1)}, bf16[2,256,384]{2,1,0:T(8,128)(2,1)S(1)}, u32[]{:S(2)}) copy-start(bf16[2,256,384]{2,1,0:T(8,128)(2,1)S(1)} %pad_maximum_fusion.3.refs_4_) | copy-start | bytes 1179652
  36.8 6.4 %copy-start.5 = (bf16[2,256,640]{2,1,0:T(8,128)(2,1)}, bf16[2,256,640]{2,1,0:T(8,128)(2,1)S(1)}, u32[]{:S(2)}) copy-start(bf16[2,256,640]{2,1,0:T(8,128)(2,1)S(1)} %collective-permute-done.2.refs_0_) | copy-start | bytes 1966084
  36.8 12.3 %collective-permute-start.5 = (bf16[2,256,384]{2,1,0:T(8,128)(2,1)S(1)}, bf16[2,256,384]{2,1,0:T(8,128)(2,1)S(1)}, u32[]{:S(2)}, u32[]{:S(2)}) collective-permute-start(bf16[2,256,384]{2,1,0:T(8,128)(2,1)S(1)} %pad_maximum_fusion.3.refs_4_), channel_id=1, source_target_pairs={{0,2},{1,3},{2,4},{3,5},{4,6},{5,7},{6,8},{7,9},{8,10},{9,11},{10,... | collective-permute-start | bytes 1179656 | tf_op jit(solution)/shard_map/ppermute | solution.py:100
  43.2 13.5 %collective-permute-start.3 = (bf16[2,256,640]{2,1,0:T(8,128)(2,1)S(1)}, bf16[2,256,640]{2,1,0:T(8,128)(2,1)S(1)}, u32[]{:S(2)}, u32[]{:S(2)}) collective-permute-start(bf16[2,256,640]{2,1,0:T(8,128)(2,1)S(1)} %get-tuple-element.24), channel_id=1, source_target_pairs={{0,1},{1,0},{2,3},{3,2},{4,5},{5,4},{6,7},{7,6},{8,9},{9,8},{10,11... | collective-permute-start | bytes 1966088 | tf_op jit(solution)/shard_map/ppermute | solution.py:135
  46.0 10.8 %collective-permute-start.4 = (bf16[2,256,640]{2,1,0:T(8,128)(2,1)S(1)}, bf16[2,256,640]{2,1,0:T(8,128)(2,1)S(1)}, u32[]{:S(2)}, u32[]{:S(2)}) collective-permute-start(bf16[2,256,640]{2,1,0:T(8,128)(2,1)S(1)} %get-tuple-element.23), channel_id=1, source_target_pairs={{0,1},{1,0},{2,3},{3,2},{4,5},{5,4},{6,7},{7,6},{8,9},{9,8},{10,11... | collective-permute-start | bytes 1966088 | tf_op jit(solution)/shard_map/ppermute | solution.py:135
  49.1 27.4 %copy-start.6 = (bf16[2,256,384]{2,1,0:T(8,128)(2,1)}, bf16[2,256,384]{2,1,0:T(8,128)(2,1)S(1)}, u32[]{:S(2)}) copy-start(bf16[2,256,384]{2,1,0:T(8,128)(2,1)S(1)} %collective-permute-done.5.refs_2_) | copy-start | bytes 1179652
  49.1 27.4 %collective-permute-start.6 = (bf16[2,256,384]{2,1,0:T(8,128)(2,1)S(1)}, bf16[2,256,384]{2,1,0:T(8,128)(2,1)S(1)}, u32[]{:S(2)}, u32[]{:S(2)}) collective-permute-start(bf16[2,256,384]{2,1,0:T(8,128)(2,1)S(1)} %collective-permute-done.5.refs_2_), channel_id=1, source_target_pairs={{0,2},{1,3},{2,4},{3,5},{4,6},{5,7},{6,8},{7,9},{8,10},{9,11},{10,... | collective-permute-start | bytes 1179656 | tf_op jit(solution)/shard_map/ppermute | solution.py:100
  56.7 1.0 copy-start
  56.7 1.2 copy-start.11
  56.7 1.4 copy-start.12
  76.5 5.2 %copy-start.7 = (bf16[2,256,384]{2,1,0:T(8,128)(2,1)}, bf16[2,256,384]{2,1,0:T(8,128)(2,1)S(1)}, u32[]{:S(2)}) copy-start(bf16[2,256,384]{2,1,0:T(8,128)(2,1)S(1)} %collective-permute-done.6.refs_0_) | copy-start | bytes 1179652
  76.6 5.8 %collective-permute-start.7 = (bf16[2,256,384]{2,1,0:T(8,128)(2,1)S(1)}, bf16[2,256,384]{2,1,0:T(8,128)(2,1)S(1)}, u32[]{:S(2)}, u32[]{:S(2)}) collective-permute-start(bf16[2,256,384]{2,1,0:T(8,128)(2,1)S(1)} %get-tuple-element.28), channel_id=1, source_target_pairs={{0,1},{1,0},{2,3},{3,2},{4,5},{5,4},{6,7},{7,6},{8,9},{9,8},{10,11... | collective-permute-start | bytes 1179656 | tf_op jit(solution)/shard_map/ppermute | solution.py:135
  80.2 2.2 %collective-permute-start.8 = (bf16[2,256,384]{2,1,0:T(8,128)(2,1)S(1)}, bf16[2,256,384]{2,1,0:T(8,128)(2,1)S(1)}, u32[]{:S(2)}, u32[]{:S(2)}) collective-permute-start(bf16[2,256,384]{2,1,0:T(8,128)(2,1)S(1)} %get-tuple-element.27), channel_id=1, source_target_pairs={{0,1},{1,0},{2,3},{3,2},{4,5},{5,4},{6,7},{7,6},{8,9},{9,8},{10,11... | collective-permute-start | bytes 1179656 | tf_op jit(solution)/shard_map/ppermute | solution.py:135
  81.9 20.4 %collective-permute-start.9 = (bf16[2,2,256,640]{3,2,1,0:T(8,128)(2,1)S(1)}, bf16[2,2,256,640]{3,2,1,0:T(8,128)(2,1)S(1)}, u32[]{:S(2)}, u32[]{:S(2)}) collective-permute-start(bf16[2,2,256,640]{3,2,1,0:T(8,128)(2,1)S(1)} %pad_maximum_fusion), channel_id=1, source_target_pairs={{0,1},{1,0},{2,3},{3,2},{4,5},{5,4},{6,7},{7,6},{8,9},{9,8},{10,11... | collective-permute-start | bytes 3932168 | tf_op jit(solution)/shard_map/ppermute | solution.py:135
  82.4 0.7 copy-start.15
  83.1 0.8 copy-start.16
  97.4 2.5 %copy-start.8 = (bf16[4,2,256,384]{3,2,1,0:T(8,128)(2,1)S(1)}, bf16[4,2,256,384]{3,2,1,0:T(8,128)(2,1)}, u32[]{:S(2)}) copy-start(bf16[4,2,256,384]{3,2,1,0:T(8,128)(2,1)} %get-tuple-element.16) | copy-start | bytes 4718596
  97.4 2.4 %collective-permute-start.12 = (bf16[2,2,256,384]{3,2,1,0:T(8,128)(2,1)S(1)}, bf16[2,2,256,384]{3,2,1,0:T(8,128)(2,1)S(1)}, u32[]{:S(2)}, u32[]{:S(2)}) collective-permute-start(bf16[2,2,256,384]{3,2,1,0:T(8,128)(2,1)S(1)} %pad_maximum_fusion.1), channel_id=1, source_target_pairs={{0,1},{1,0},{2,3},{3,2},{4,5},{5,4},{6,7},{7,6},{8,9},{9,8},{10,11... | collective-permute-start | bytes 2359304 | tf_op jit(solution)/shard_map/ppermute | solution.py:135
  100.1 2.4 %copy-start.3 = (bf16[4,2,256,640]{3,2,1,0:T(8,128)(2,1)S(1)}, bf16[4,2,256,640]{3,2,1,0:T(8,128)(2,1)}, u32[]{:S(2)}) copy-start(bf16[4,2,256,640]{3,2,1,0:T(8,128)(2,1)} %get-tuple-element.14) | copy-start | bytes 7864324
  100.1 14.8 %collective-permute-start.13 = (bf16[2,256,384]{2,1,0:T(8,128)(2,1)S(1)}, bf16[2,256,384]{2,1,0:T(8,128)(2,1)S(1)}, u32[]{:S(2)}, u32[]{:S(2)}) collective-permute-start(bf16[2,256,384]{2,1,0:T(8,128)(2,1)S(1)} %fusion.10), channel_id=1, source_target_pairs={{2,0},{3,1},{4,2},{5,3},{6,4},{7,5},{8,6},{9,7},{10,8},{11,9},{12,... | collective-permute-start | bytes 1179656 | tf_op jit(solution)/shard_map/ppermute | solution.py:100
  102.6 26.3 %collective-permute-start.10 = (bf16[2,256,640]{2,1,0:T(8,128)(2,1)S(1)}, bf16[2,256,640]{2,1,0:T(8,128)(2,1)S(1)}, u32[]{:S(2)}, u32[]{:S(2)}) collective-permute-start(bf16[2,256,640]{2,1,0:T(8,128)(2,1)S(1)} %fusion.9), channel_id=1, source_target_pairs={{2,0},{3,1},{4,2},{5,3},{6,4},{7,5},{8,6},{9,7},{10,8},{11,9},{12,... | collective-permute-start | bytes 1966088 | tf_op jit(solution)/shard_map/ppermute | solution.py:100
  115.1 16.2 %copy-start.13 = (bf16[256,1280]{1,0:T(8,128)(2,1)S(1)}, bf16[256,1280]{1,0:T(8,128)(2,1)}, u32[]{:S(2)}) copy-start(bf16[256,1280]{1,0:T(8,128)(2,1)} %get-tuple-element.10) | copy-start | bytes 1966084
  115.1 16.2 %copy-start.14 = (bf16[256,768]{1,0:T(8,128)(2,1)S(1)}, bf16[256,768]{1,0:T(8,128)(2,1)}, u32[]{:S(2)}) copy-start(bf16[256,768]{1,0:T(8,128)(2,1)} %get-tuple-element.12) | copy-start | bytes 1179652
  115.1 22.2 %collective-permute-start.14 = (bf16[2,256,384]{2,1,0:T(8,128)(2,1)S(1)}, bf16[2,256,384]{2,1,0:T(8,128)(2,1)S(1)}, u32[]{:S(2)}, u32[]{:S(2)}) collective-permute-start(bf16[2,256,384]{2,1,0:T(8,128)(2,1)S(1)} %fusion.8), channel_id=1, source_target_pairs={{2,0},{3,1},{4,2},{5,3},{6,4},{7,5},{8,6},{9,7},{10,8},{11,9},{12,... | collective-permute-start | bytes 1179656 | tf_op jit(solution)/shard_map/ppermute | solution.py:100
  129.2 8.2 %copy-start.10 = (f32[2,256,384]{2,1,0:T(8,128)S(1)}, f32[2,256,384]{2,1,0:T(8,128)}, u32[]{:S(2)}) copy-start(f32[2,256,384]{2,1,0:T(8,128)} %get-tuple-element.15) | copy-start | bytes 2359300
  129.2 22.2 %collective-permute-start.11 = (bf16[2,256,640]{2,1,0:T(8,128)(2,1)S(1)}, bf16[2,256,640]{2,1,0:T(8,128)(2,1)S(1)}, u32[]{:S(2)}, u32[]{:S(2)}) collective-permute-start(bf16[2,256,640]{2,1,0:T(8,128)(2,1)S(1)} %fusion.2), channel_id=1, source_target_pairs={{2,0},{3,1},{4,2},{5,3},{6,4},{7,5},{8,6},{9,7},{10,8},{11,9},{12,... | collective-permute-start | bytes 1966088 | tf_op jit(solution)/shard_map/ppermute | solution.py:100
  137.4 14.0 %copy-start.9 = (f32[2,256,640]{2,1,0:T(8,128)S(1)}, f32[2,256,640]{2,1,0:T(8,128)}, u32[]{:S(2)}) copy-start(f32[2,256,640]{2,1,0:T(8,128)} %get-tuple-element.13) | copy-start | bytes 3932164
where the time goes:
time: 154 us; the launch traced here: 153 us
  waiting for transfers between devices  66.2 us (43%)
  starting transfers between devices  41.2 us (27%)
  Pallas kernels  30.6 us (20%)
  local copies, waits for them, and re-layouts  7.85 us (5%)
  other arithmetic  6.57 us (4%)
    ppermute x8, waiting for transfers between devices, shifted(): lax.ppermute(value, axis, [(source, source + steps) for source in range(i...  64 us
    pallas_call x2, Pallas kernels, attention_back(): pl.pallas_call(attention_back_kernel, grid_spec=grid_spec, out_shape=[jax...  30.6 us
    ppermute x8, starting transfers between devices, shifted(): lax.ppermute(value, axis, [(source, source + steps) for source in range(i...  28.3 us
    ppermute x6, starting transfers between devices, partner(): return lax.ppermute(value, 'ctx', [(i, i ^ 1) for i in range(count)])  7.23 us
    ppermute x1, starting transfers between devices, passed_along(): lax.ppermute(shard, axis, [(i, (i + by) % count) for i in range(count)])  5.65 us
  transfers between devices with their start and end apart: 15, of which 8 were waited for; matrix products, arithmetic and copies ran while one was open for 6% of the time, Pallas kernels for 20%

commit v1 on v0

--- a/solution.py
+++ b/solution.py
@@ -8,7 +8,7 @@
 
 WINDOW = 1024
 KV_HEADS = 8
-CHUNK_GROUPS = (5, 3)
+CHUNKS = 2
 GROUP = 2
 
 
@@ -126,7 +126,13 @@
     query_pos = first_pos + jnp.arange(count_rows, dtype=jnp.int32)
     key_pos = first_pos - WINDOW + jnp.arange(WINDOW + count_rows, dtype=jnp.int32)
     allowed = window_mask(query_pos, key_pos, doc_lengths).astype(jnp.float32)
+    chunk_groups = KV_HEADS // CHUNKS
+    chunk_width = chunk_groups * head_size
     mask = allowed.astype(jnp.bfloat16)
+
+    def own_pair_of(chunk):
+        cols = slice(chunk * chunk_width, (chunk + 1) * chunk_width)
+        return jnp.stack([keys_here[:, cols], values_here[:, cols]])
 
     odd = (rank_here % 2) == 1
 
@@ -151,26 +157,22 @@
         arrived = shifted((arrived + to_two).astype(jnp.bfloat16), "ctx", -2).astype(jnp.float32)
         return (own + (arrived + direct)).astype(jnp.bfloat16)
 
-    firsts = [sum(CHUNK_GROUPS[:chunk]) for chunk in range(len(CHUNK_GROUPS))]
+    window_a = forward(own_pair_of(0))
+    own_b = lax.optimization_barrier((own_pair_of(1), window_a[0]))[0]
+    window_b = forward(own_b)
+    windows = [window_a, window_b]
+
     query_parts = []
-    totals = []
-    windows = []
-    after = None
-    for chunk, groups in enumerate(CHUNK_GROUPS):
-        cols = slice(firsts[chunk] * head_size, (firsts[chunk] + groups) * head_size)
-        own_pair = jnp.stack([keys_here[:, cols], values_here[:, cols]])
-        if after is not None:
-            own_pair = lax.optimization_barrier((own_pair, after))[0]
-        windows.append(forward(own_pair))
-        after = windows[-1][0]
-    for chunk, groups in enumerate(CHUNK_GROUPS):
+    results = []
+    for chunk in range(CHUNKS):
         query_part, far, own = attention_back(
-            queries, arriving, windows[chunk], mask, firsts[chunk], 0, groups
+            queries, arriving, windows[chunk], mask, chunk * chunk_groups, 0, chunk_groups
         )
         query_parts.append(query_part)
-        totals.append(backward(far, own))
+        results.append((far, own))
     query_back = jnp.concatenate(query_parts, axis=1)
 
+    totals = [backward(far, own) for far, own in results]
     return (
         query_back[None],
         jnp.concatenate([total[0] for total in totals], axis=1)[None],

time: 154 us -> 161 us (1.045)
  other arithmetic: 6.57 us -> 10.4 us
  waiting for transfers between devices: 66.2 us -> 68.1 us
    ppermute x8, waiting for transfers between devices: 64 us -> 68.1 us  [shifted(): lax.ppermute(value, axis, [(source, source + steps) for source in range(i...]
    select_n x2, other arithmetic: 0.23 us -> 2.46 us  [forward(): minus_one = partner(jnp.where(odd, minus_two, own))]
    ppermute x6, waiting for transfers between devices: 2.21 us -> 0.02 us  [partner(): return lax.ppermute(value, 'ctx', [(i, i ^ 1) for i in range(count)])]
    unnamed x36 -> x30, local copies, waits for them, and re-layouts: 2.39 us -> 3.36 us
  transfers between devices with their start and end apart: 15 -> 15, of which waited for: 8 -> 8; matrix products, arithmetic and copies ran while one was open for 6% -> 7% of each run, Pallas kernels for 20% -> 19%
where the time goes in v1:
time: 161 us; the launch traced here: 160 us
  waiting for transfers between devices  68.1 us (42%)
  starting transfers between devices  41.7 us (26%)
  Pallas kernels  30.5 us (19%)
  other arithmetic  10.4 us (6%)
  local copies, waits for them, and re-layouts  8.54 us (5%)
    ppermute x8, waiting for transfers between devices, shifted(): lax.ppermute(value, axis, [(source, source + steps) for source in range(i...  68.1 us
    pallas_call x2, Pallas kernels, attention_back(): pl.pallas_call(attention_back_kernel, grid_spec=grid_spec, out_shape=[jax...  30.5 us
    ppermute x8, starting transfers between devices, shifted(): lax.ppermute(value, axis, [(source, source + steps) for source in range(i...  28.2 us
    ppermute x6, starting transfers between devices, partner(): return lax.ppermute(value, 'ctx', [(i, i ^ 1) for i in range(count)])  7.82 us
    ppermute x1, starting transfers between devices, passed_along(): lax.ppermute(shard, axis, [(i, (i + by) % count) for i in range(count)])  5.65 us
    unnamed x30, local copies, waits for them, and re-layouts  3.36 us
  transfers between devices with their start and end apart: 15, of which 8 were waited for; matrix products, arithmetic and copies ran while one was open for 7% of the time, Pallas kernels for 19%

profile of v1, /device:TPU:25, one launch (start us, length us, event | category | flops | bytes accessed | tf_op | source)
XLA Modules:
  0.0 160.2 jit_solution(10699069826109031058)
XLA Ops:
  0.6 2.0 %slice_bitcast_fusion.6 = (bf16[1,256,512]{2,1,0:T(8,128)(2,1)S(1)}, bf16[1,256,512]{2,1,0:T(8,128)(2,1)S(1)}, bf16[1,256,512]{2,1,0:T(8,128)(2,1)}, bf16[1,256,512]{2,1,0:T(8,128)(2,1)S(1)}) fusion(bf16[256,1024]{1,0:T(8,128)(2,1)} %bitcast.56, bf16[256,1024]{1,0:T(8,128)(2,1)} %bitcast.57), kind=kLoop, calls=%fused_computation.37 | loop fusion | bytes 2097152 | tf_op jit(solution)/shard_map/stack | solution.py:135
  2.6 0.1 pad_maximum_fusion.2.refs_4_
  2.7 2.8 %collective-permute-start.1 = (bf16[2,256,512]{2,1,0:T(8,128)(2,1)S(1)}, bf16[2,256,512]{2,1,0:T(8,128)(2,1)S(1)}, u32[]{:S(2)}, u32[]{:S(2)}) collective-permute-start(bf16[2,256,512]{2,1,0:T(8,128)(2,1)S(1)} %pad_maximum_fusion.2.refs_4_), channel_id=1, source_target_pairs={{0,2},{1,3},{2,4},{3,5},{4,6},{5,7},{6,8},{7,9},{8,10},{9,11},{10,... | collective-permute-start | bytes 1572872 | tf_op jit(solution)/shard_map/ppermute | solution.py:100
  5.5 11.9 %collective-permute-done.1.refs_2_ = bf16[2,256,512]{2,1,0:T(8,128)(2,1)S(1)} collective-permute-done((bf16[2,256,512]{2,1,0:T(8,128)(2,1)S(1)}, bf16[2,256,512]{2,1,0:T(8,128)(2,1)S(1)}, u32[]{:S(2)}, u32[]{:S(2)}) %collective-permute-start.1) | collective-permute-done | bytes 524320 | tf_op jit(solution)/shard_map/ppermute | solution.py:100
  17.4 4.9 %collective-permute-start.2 = (bf16[2,256,512]{2,1,0:T(8,128)(2,1)S(1)}, bf16[2,256,512]{2,1,0:T(8,128)(2,1)}, u32[]{:S(2)}, u32[]{:S(2)}) collective-permute-start(bf16[2,256,512]{2,1,0:T(8,128)(2,1)S(1)} %collective-permute-done.1.refs_2_), channel_id=1, source_target_pairs={{0,2},{1,3},{2,4},{3,5},{4,6},{5,7},{6,8},{7,9},{8,10},{9,11},{10,... | collective-permute-start | bytes 1572872 | tf_op jit(solution)/shard_map/ppermute | solution.py:100
  22.3 5.7 %collective-permute-start = (bf16[1,256,2048]{2,1,0:T(8,128)(2,1)}, bf16[1,256,2048]{2,1,0:T(8,128)(2,1)S(1)}, u32[]{:S(2)}, u32[]{:S(2)}) collective-permute-start(bf16[1,256,2048]{2,1,0:T(8,128)(2,1)} %param.10), channel_id=1, source_target_pairs={{0,224},{32,0},{64,32},{96,64},{128,96},{160,128},{192,160},{224,1... | collective-permute-start | bytes 3145736 | tf_op jit(solution)/shard_map/ppermute | solution.py:94
  27.9 0.0 copy-done.14
  27.9 0.2 reduce-window.8
  28.1 1.0 pad_maximum_fusion.3.refs_4_
  29.1 2.9 %collective-permute-done.2.refs_0_ = bf16[2,256,512]{2,1,0:T(8,128)(2,1)} collective-permute-done((bf16[2,256,512]{2,1,0:T(8,128)(2,1)S(1)}, bf16[2,256,512]{2,1,0:T(8,128)(2,1)}, u32[]{:S(2)}, u32[]{:S(2)}) %collective-permute-start.2) | collective-permute-done | bytes 524320 | tf_op jit(solution)/shard_map/ppermute | solution.py:100
  32.0 6.3 %collective-permute-start.5 = (bf16[2,256,512]{2,1,0:T(8,128)(2,1)S(1)}, bf16[2,256,512]{2,1,0:T(8,128)(2,1)}, u32[]{:S(2)}, u32[]{:S(2)}) collective-permute-start(bf16[2,256,512]{2,1,0:T(8,128)(2,1)S(1)} %pad_maximum_fusion.3.refs_4_), channel_id=1, source_target_pairs={{0,2},{1,3},{2,4},{3,5},{4,6},{5,7},{6,8},{7,9},{8,10},{9,11},{10,... | collective-permute-start | bytes 1572872 | tf_op jit(solution)/shard_map/ppermute | solution.py:100
  38.4 0.1 convert_reduce_fusion.1
  38.4 0.1 convert_reduce_fusion
  38.6 8.6 %collective-permute-done.5.refs_2_ = bf16[2,256,512]{2,1,0:T(8,128)(2,1)} collective-permute-done((bf16[2,256,512]{2,1,0:T(8,128)(2,1)S(1)}, bf16[2,256,512]{2,1,0:T(8,128)(2,1)}, u32[]{:S(2)}, u32[]{:S(2)}) %collective-permute-start.5) | collective-permute-done | bytes 524320 | tf_op jit(solution)/shard_map/ppermute | solution.py:100
  47.2 6.3 %collective-permute-start.6 = (bf16[2,256,512]{2,1,0:T(8,128)(2,1)}, bf16[2,256,512]{2,1,0:T(8,128)(2,1)S(1)}, u32[]{:S(2)}, u32[]{:S(2)}) collective-permute-start(bf16[2,256,512]{2,1,0:T(8,128)(2,1)} %collective-permute-done.5.refs_2_), channel_id=1, source_target_pairs={{0,2},{1,3},{2,4},{3,5},{4,6},{5,7},{6,8},{7,9},{8,10},{9,11},{10,... | collective-permute-start | bytes 1572872 | tf_op jit(solution)/shard_map/ppermute | solution.py:100
  53.5 1.1 broadcast_select_fusion.2
  54.7 2.6 %collective-permute-start.3 = (bf16[2,256,512]{2,1,0:T(8,128)(2,1)S(1)}, bf16[2,256,512]{2,1,0:T(8,128)(2,1)S(1)}, u32[]{:S(2)}, u32[]{:S(2)}) collective-permute-start(bf16[2,256,512]{2,1,0:T(8,128)(2,1)S(1)} %get-tuple-element.26), channel_id=1, source_target_pairs={{0,1},{1,0},{2,3},{3,2},{4,5},{5,4},{6,7},{7,6},{8,9},{9,8},{10,11... | collective-permute-start | bytes 1572872 | tf_op jit(solution)/shard_map/ppermute | solution.py:141
  57.2 0.1 collective-permute-start.4
  57.3 1.4 convert_convert_fusion.refs_5_
  58.7 0.0 copy-done.5
  58.8 3.1 %collective-permute-done.6.refs_0_ = bf16[2,256,512]{2,1,0:T(8,128)(2,1)S(1)} collective-permute-done((bf16[2,256,512]{2,1,0:T(8,128)(2,1)}, bf16[2,256,512]{2,1,0:T(8,128)(2,1)S(1)}, u32[]{:S(2)}, u32[]{:S(2)}) %collective-permute-start.6) | collective-permute-done | bytes 524320 | tf_op jit(solution)/shard_map/ppermute | solution.py:100
  61.9 1.3 broadcast_select_fusion
  63.2 4.2 %collective-permute-start.7 = (bf16[2,256,512]{2,1,0:T(8,128)(2,1)S(1)}, bf16[2,256,512]{2,1,0:T(8,128)(2,1)S(1)}, u32[]{:S(2)}, u32[]{:S(2)}) collective-permute-start(bf16[2,256,512]{2,1,0:T(8,128)(2,1)S(1)} %get-tuple-element.28), channel_id=1, source_target_pairs={{0,1},{1,0},{2,3},{3,2},{4,5},{5,4},{6,7},{7,6},{8,9},{9,8},{10,11... | collective-permute-start | bytes 1572872 | tf_op jit(solution)/shard_map/ppermute | solution.py:141
  67.4 0.1 collective-permute-start.8
  67.5 0.0 collective-permute-done
  67.5 0.0 collective-permute-done.3.refs_1_
  67.5 0.0 copy-start.12
  67.5 0.0 collective-permute-done.4.refs_3_
  67.5 0.8 copy-done.12
  68.3 0.8 copy-done.13
  69.1 0.6 call_exported.0.at_ref
  69.7 15.2 %shard_map.94 = (bf16[256,1024]{1,0:T(8,128)(2,1)}, bf16[4,2,256,512]{3,2,1,0:T(8,128)(2,1)}, f32[2,256,512]{2,1,0:T(8,128)}) custom-call(s32[2]{0:T(128)} %call_exported.0.at_ref, bf16[256,2048]{1,0:T(8,128)(2,1)} %bitcast.52, bf16[256,2048]{1,0:T(8,128)(2,1)} %bitcast.54, bf16[2,256,512]{2,1,0:T(8,128)(2,1)} %collective-permute-done.2.refs_0_, ...), custom_call_target="tpu_custom_call" | custom-call | tf_op jit(solution)/shard_map/pallas_call | solution.py:80
  84.9 1.3 fusion.11
  86.2 0.1 pad_maximum_fusion
  86.3 0.5 collective-permute-start.9
  86.8 0.0 collective-permute-done.7.refs_1_
  86.8 0.0 collective-permute-done.8.refs_3_
  86.8 0.8 copy-done.11
  87.6 15.3 %shard_map.95 = (bf16[256,1024]{1,0:T(8,128)(2,1)}, bf16[4,2,256,512]{3,2,1,0:T(8,128)(2,1)}, f32[2,256,512]{2,1,0:T(8,128)}) custom-call(s32[2]{0:T(128)} %constant.39.clone.at_ref, bf16[256,2048]{1,0:T(8,128)(2,1)} %bitcast.53, bf16[256,2048]{1,0:T(8,128)(2,1)} %bitcast.55, bf16[2,256,512]{2,1,0:T(8,128)(2,1)} %copy-done.6, ...), custom_call_target="tpu_custom_call" | custom-call | tf_op jit(solution)/shard_map/pallas_call | solution.py:80
  102.9 1.3 fusion.12
  104.1 0.1 pad_maximum_fusion.1
  104.3 0.4 collective-permute-start.12
  104.6 0.0 collective-permute-done.9
  104.6 0.3 convert_element_type.75
  104.9 0.9 copy-done.2
  105.8 0.2 fusion.9
  106.0 2.1 %collective-permute-start.10 = (bf16[2,256,512]{2,1,0:T(8,128)(2,1)S(1)}, bf16[2,256,512]{2,1,0:T(8,128)(2,1)S(1)}, u32[]{:S(2)}, u32[]{:S(2)}) collective-permute-start(bf16[2,256,512]{2,1,0:T(8,128)(2,1)S(1)} %fusion.9), channel_id=1, source_target_pairs={{2,0},{3,1},{4,2},{5,3},{6,4},{7,5},{8,6},{9,7},{10,8},{11,9},{12,... | collective-permute-start | bytes 1572872 | tf_op jit(solution)/shard_map/ppermute | solution.py:100
  108.1 0.0 collective-permute-done.12
  108.1 0.3 convert_element_type.84
  108.4 0.2 fusion.10
  108.6 2.1 %collective-permute-start.13 = (bf16[2,256,512]{2,1,0:T(8,128)(2,1)S(1)}, bf16[2,256,512]{2,1,0:T(8,128)(2,1)S(1)}, u32[]{:S(2)}, u32[]{:S(2)}) collective-permute-start(bf16[2,256,512]{2,1,0:T(8,128)(2,1)S(1)} %fusion.10), channel_id=1, source_target_pairs={{2,0},{3,1},{4,2},{5,3},{6,4},{7,5},{8,6},{9,7},{10,8},{11,9},{12,... | collective-permute-start | bytes 1572872 | tf_op jit(solution)/shard_map/ppermute | solution.py:100
  110.7 13.8 %collective-permute-done.10 = bf16[2,256,512]{2,1,0:T(8,128)(2,1)S(1)} collective-permute-done((bf16[2,256,512]{2,1,0:T(8,128)(2,1)S(1)}, bf16[2,256,512]{2,1,0:T(8,128)(2,1)S(1)}, u32[]{:S(2)}, u32[]{:S(2)}) %collective-permute-start.10) | collective-permute-done | bytes 524320 | tf_op jit(solution)/shard_map/ppermute | solution.py:100
  124.4 0.3 fusion.8
  124.8 1.9 %collective-permute-start.11 = (bf16[2,256,512]{2,1,0:T(8,128)(2,1)S(1)}, bf16[2,256,512]{2,1,0:T(8,128)(2,1)S(1)}, u32[]{:S(2)}, u32[]{:S(2)}) collective-permute-start(bf16[2,256,512]{2,1,0:T(8,128)(2,1)S(1)} %fusion.8), channel_id=1, source_target_pairs={{2,0},{3,1},{4,2},{5,3},{6,4},{7,5},{8,6},{9,7},{10,8},{11,9},{12,... | collective-permute-start | bytes 1572872 | tf_op jit(solution)/shard_map/ppermute | solution.py:100
  126.7 1.1 maximum_bitcast_fusion
  127.8 7.9 %collective-permute-done.13 = bf16[2,256,512]{2,1,0:T(8,128)(2,1)S(1)} collective-permute-done((bf16[2,256,512]{2,1,0:T(8,128)(2,1)S(1)}, bf16[2,256,512]{2,1,0:T(8,128)(2,1)S(1)}, u32[]{:S(2)}, u32[]{:S(2)}) %collective-permute-start.13) | collective-permute-done | bytes 524320 | tf_op jit(solution)/shard_map/ppermute | solution.py:100
  135.7 0.3 fusion.5
  136.0 1.9 %collective-permute-start.14 = (bf16[2,256,512]{2,1,0:T(8,128)(2,1)S(1)}, bf16[2,256,512]{2,1,0:T(8,128)(2,1)S(1)}, u32[]{:S(2)}, u32[]{:S(2)}) collective-permute-start(bf16[2,256,512]{2,1,0:T(8,128)(2,1)S(1)} %fusion.5), channel_id=1, source_target_pairs={{2,0},{3,1},{4,2},{5,3},{6,4},{7,5},{8,6},{9,7},{10,8},{11,9},{12,... | collective-permute-start | bytes 1572872 | tf_op jit(solution)/shard_map/ppermute | solution.py:100
  138.0 9.0 %collective-permute-done.11 = bf16[2,256,512]{2,1,0:T(8,128)(2,1)S(1)} collective-permute-done((bf16[2,256,512]{2,1,0:T(8,128)(2,1)S(1)}, bf16[2,256,512]{2,1,0:T(8,128)(2,1)S(1)}, u32[]{:S(2)}, u32[]{:S(2)}) %collective-permute-start.11) | collective-permute-done | bytes 524320 | tf_op jit(solution)/shard_map/ppermute | solution.py:100
  146.9 0.3 fusion.7
  147.3 10.9 %collective-permute-done.14 = bf16[2,256,512]{2,1,0:T(8,128)(2,1)S(1)} collective-permute-done((bf16[2,256,512]{2,1,0:T(8,128)(2,1)S(1)}, bf16[2,256,512]{2,1,0:T(8,128)(2,1)S(1)}, u32[]{:S(2)}, u32[]{:S(2)}) %collective-permute-start.14) | collective-permute-done | bytes 524320 | tf_op jit(solution)/shard_map/ppermute | solution.py:100
  158.2 0.3 fusion.4
  158.5 0.9 maximum_bitcast_fusion.2
  159.4 0.9 maximum_bitcast_fusion.1
  (28 shorter events, 0.1 us)
Async XLA Ops:
  0.6 27.3 %copy-start.14 = (s32[4]{0:T(128)S(1)}, s32[4]{0:T(128)}, u32[]{:S(2)}) copy-start(s32[4]{0:T(128)} %param.11) | copy-start | bytes 52
  2.7 56.1 %copy-start.4 = (bf16[2,256,512]{2,1,0:T(8,128)(2,1)}, bf16[2,256,512]{2,1,0:T(8,128)(2,1)S(1)}, u32[]{:S(2)}) copy-start(bf16[2,256,512]{2,1,0:T(8,128)(2,1)S(1)} %pad_maximum_fusion.2.refs_4_) | copy-start | bytes 1572868
  2.7 14.7 %collective-permute-start.1 = (bf16[2,256,512]{2,1,0:T(8,128)(2,1)S(1)}, bf16[2,256,512]{2,1,0:T(8,128)(2,1)S(1)}, u32[]{:S(2)}, u32[]{:S(2)}) collective-permute-start(bf16[2,256,512]{2,1,0:T(8,128)(2,1)S(1)} %pad_maximum_fusion.2.refs_4_), channel_id=1, source_target_pairs={{0,2},{1,3},{2,4},{3,5},{4,6},{5,7},{6,8},{7,9},{8,10},{9,11},{10,... | collective-permute-start | bytes 1572872 | tf_op jit(solution)/shard_map/ppermute | solution.py:100
  17.4 41.4 %copy-start.5 = (bf16[2,256,512]{2,1,0:T(8,128)(2,1)}, bf16[2,256,512]{2,1,0:T(8,128)(2,1)S(1)}, u32[]{:S(2)}) copy-start(bf16[2,256,512]{2,1,0:T(8,128)(2,1)S(1)} %collective-permute-done.1.refs_2_) | copy-start | bytes 1572868
  17.4 14.6 %collective-permute-start.2 = (bf16[2,256,512]{2,1,0:T(8,128)(2,1)S(1)}, bf16[2,256,512]{2,1,0:T(8,128)(2,1)}, u32[]{:S(2)}, u32[]{:S(2)}) collective-permute-start(bf16[2,256,512]{2,1,0:T(8,128)(2,1)S(1)} %collective-permute-done.1.refs_2_), channel_id=1, source_target_pairs={{0,2},{1,3},{2,4},{3,5},{4,6},{5,7},{6,8},{7,9},{8,10},{9,11},{10,... | collective-permute-start | bytes 1572872 | tf_op jit(solution)/shard_map/ppermute | solution.py:100
  22.3 45.2 %collective-permute-start = (bf16[1,256,2048]{2,1,0:T(8,128)(2,1)}, bf16[1,256,2048]{2,1,0:T(8,128)(2,1)S(1)}, u32[]{:S(2)}, u32[]{:S(2)}) collective-permute-start(bf16[1,256,2048]{2,1,0:T(8,128)(2,1)} %param.10), channel_id=1, source_target_pairs={{0,224},{32,0},{64,32},{96,64},{128,96},{160,128},{192,160},{224,1... | collective-permute-start | bytes 3145736 | tf_op jit(solution)/shard_map/ppermute | solution.py:94
  29.1 34.1 %copy-start = (bf16[2,256,512]{2,1,0:T(8,128)(2,1)}, bf16[2,256,512]{2,1,0:T(8,128)(2,1)S(1)}, u32[]{:S(2)}) copy-start(bf16[2,256,512]{2,1,0:T(8,128)(2,1)S(1)} %pad_maximum_fusion.3.refs_4_) | copy-start | bytes 1572868
  32.0 15.2 %collective-permute-start.5 = (bf16[2,256,512]{2,1,0:T(8,128)(2,1)S(1)}, bf16[2,256,512]{2,1,0:T(8,128)(2,1)}, u32[]{:S(2)}, u32[]{:S(2)}) collective-permute-start(bf16[2,256,512]{2,1,0:T(8,128)(2,1)S(1)} %pad_maximum_fusion.3.refs_4_), channel_id=1, source_target_pairs={{0,2},{1,3},{2,4},{3,5},{4,6},{5,7},{6,8},{7,9},{8,10},{9,11},{10,... | collective-permute-start | bytes 1572872 | tf_op jit(solution)/shard_map/ppermute | solution.py:100
  47.2 14.7 %collective-permute-start.6 = (bf16[2,256,512]{2,1,0:T(8,128)(2,1)}, bf16[2,256,512]{2,1,0:T(8,128)(2,1)S(1)}, u32[]{:S(2)}, u32[]{:S(2)}) collective-permute-start(bf16[2,256,512]{2,1,0:T(8,128)(2,1)} %collective-permute-done.5.refs_2_), channel_id=1, source_target_pairs={{0,2},{1,3},{2,4},{3,5},{4,6},{5,7},{6,8},{7,9},{8,10},{9,11},{10,... | collective-permute-start | bytes 1572872 | tf_op jit(solution)/shard_map/ppermute | solution.py:100
  54.7 12.8 %collective-permute-start.3 = (bf16[2,256,512]{2,1,0:T(8,128)(2,1)S(1)}, bf16[2,256,512]{2,1,0:T(8,128)(2,1)S(1)}, u32[]{:S(2)}, u32[]{:S(2)}) collective-permute-start(bf16[2,256,512]{2,1,0:T(8,128)(2,1)S(1)} %get-tuple-element.26), channel_id=1, source_target_pairs={{0,1},{1,0},{2,3},{3,2},{4,5},{5,4},{6,7},{7,6},{8,9},{9,8},{10,11... | collective-permute-start | bytes 1572872 | tf_op jit(solution)/shard_map/ppermute | solution.py:141
  57.2 10.3 %collective-permute-start.4 = (bf16[2,256,512]{2,1,0:T(8,128)(2,1)S(1)}, bf16[2,256,512]{2,1,0:T(8,128)(2,1)S(1)}, u32[]{:S(2)}, u32[]{:S(2)}) collective-permute-start(bf16[2,256,512]{2,1,0:T(8,128)(2,1)S(1)} %get-tuple-element.25), channel_id=1, source_target_pairs={{0,1},{1,0},{2,3},{3,2},{4,5},{5,4},{6,7},{7,6},{8,9},{9,8},{10,11... | collective-permute-start | bytes 1572872 | tf_op jit(solution)/shard_map/ppermute | solution.py:141
  61.9 23.1 %copy-start.6 = (bf16[2,256,512]{2,1,0:T(8,128)(2,1)}, bf16[2,256,512]{2,1,0:T(8,128)(2,1)S(1)}, u32[]{:S(2)}) copy-start(bf16[2,256,512]{2,1,0:T(8,128)(2,1)S(1)} %collective-permute-done.6.refs_0_) | copy-start | bytes 1572868
  63.2 23.6 %collective-permute-start.7 = (bf16[2,256,512]{2,1,0:T(8,128)(2,1)S(1)}, bf16[2,256,512]{2,1,0:T(8,128)(2,1)S(1)}, u32[]{:S(2)}, u32[]{:S(2)}) collective-permute-start(bf16[2,256,512]{2,1,0:T(8,128)(2,1)S(1)} %get-tuple-element.28), channel_id=1, source_target_pairs={{0,1},{1,0},{2,3},{3,2},{4,5},{5,4},{6,7},{7,6},{8,9},{9,8},{10,11... | collective-permute-start | bytes 1572872 | tf_op jit(solution)/shard_map/ppermute | solution.py:141
  67.4 19.5 %collective-permute-start.8 = (bf16[2,256,512]{2,1,0:T(8,128)(2,1)S(1)}, bf16[2,256,512]{2,1,0:T(8,128)(2,1)}, u32[]{:S(2)}, u32[]{:S(2)}) collective-permute-start(bf16[2,256,512]{2,1,0:T(8,128)(2,1)S(1)} %get-tuple-element.27), channel_id=1, source_target_pairs={{0,1},{1,0},{2,3},{3,2},{4,5},{5,4},{6,7},{7,6},{8,9},{9,8},{10,11... | collective-permute-start | bytes 1572872 | tf_op jit(solution)/shard_map/ppermute | solution.py:141
  67.5 2.2 %copy-start.1 = (bf16[1,256,2048]{2,1,0:T(8,128)(2,1)}, bf16[1,256,2048]{2,1,0:T(8,128)(2,1)S(1)}, u32[]{:S(2)}) copy-start(bf16[1,256,2048]{2,1,0:T(8,128)(2,1)S(1)} %collective-permute-done) | copy-start | bytes 3145732
  67.5 0.8 copy-start.12
  68.3 0.8 copy-start.13
  86.3 18.3 %collective-permute-start.9 = (bf16[2,2,256,512]{3,2,1,0:T(8,128)(2,1)S(1)}, bf16[2,2,256,512]{3,2,1,0:T(8,128)(2,1)S(1)}, u32[]{:S(2)}, u32[]{:S(2)}) collective-permute-start(bf16[2,2,256,512]{3,2,1,0:T(8,128)(2,1)S(1)} %pad_maximum_fusion), channel_id=1, source_target_pairs={{0,1},{1,0},{2,3},{3,2},{4,5},{5,4},{6,7},{7,6},{8,9},{9,8},{10,11... | collective-permute-start | bytes 3145736 | tf_op jit(solution)/shard_map/ppermute | solution.py:141
  86.8 0.8 copy-start.11
  104.3 1.6 copy-start.2
  104.3 3.8 %collective-permute-start.12 = (bf16[2,2,256,512]{3,2,1,0:T(8,128)(2,1)S(1)}, bf16[2,2,256,512]{3,2,1,0:T(8,128)(2,1)S(1)}, u32[]{:S(2)}, u32[]{:S(2)}) collective-permute-start(bf16[2,2,256,512]{3,2,1,0:T(8,128)(2,1)S(1)} %pad_maximum_fusion.1), channel_id=1, source_target_pairs={{0,1},{1,0},{2,3},{3,2},{4,5},{5,4},{6,7},{7,6},{8,9},{9,8},{10,11... | collective-permute-start | bytes 3145736 | tf_op jit(solution)/shard_map/ppermute | solution.py:141
  106.0 2.4 %copy-start.3 = (bf16[4,2,256,512]{3,2,1,0:T(8,128)(2,1)S(1)}, bf16[4,2,256,512]{3,2,1,0:T(8,128)(2,1)}, u32[]{:S(2)}) copy-start(bf16[4,2,256,512]{3,2,1,0:T(8,128)(2,1)} %get-tuple-element.16) | copy-start | bytes 6291460
  106.0 18.4 %collective-permute-start.10 = (bf16[2,256,512]{2,1,0:T(8,128)(2,1)S(1)}, bf16[2,256,512]{2,1,0:T(8,128)(2,1)S(1)}, u32[]{:S(2)}, u32[]{:S(2)}) collective-permute-start(bf16[2,256,512]{2,1,0:T(8,128)(2,1)S(1)} %fusion.9), channel_id=1, source_target_pairs={{2,0},{3,1},{4,2},{5,3},{6,4},{7,5},{8,6},{9,7},{10,8},{11,9},{12,... | collective-permute-start | bytes 1572872 | tf_op jit(solution)/shard_map/ppermute | solution.py:100
  108.6 18.2 %copy-start.9 = (bf16[256,1024]{1,0:T(8,128)(2,1)S(1)}, bf16[256,1024]{1,0:T(8,128)(2,1)}, u32[]{:S(2)}) copy-start(bf16[256,1024]{1,0:T(8,128)(2,1)} %get-tuple-element.10) | copy-start | bytes 1572868
  108.6 18.2 %copy-start.10 = (bf16[256,1024]{1,0:T(8,128)(2,1)S(1)}, bf16[256,1024]{1,0:T(8,128)(2,1)}, u32[]{:S(2)}) copy-start(bf16[256,1024]{1,0:T(8,128)(2,1)} %get-tuple-element.12) | copy-start | bytes 1572868
  108.6 27.1 %collective-permute-start.13 = (bf16[2,256,512]{2,1,0:T(8,128)(2,1)S(1)}, bf16[2,256,512]{2,1,0:T(8,128)(2,1)S(1)}, u32[]{:S(2)}, u32[]{:S(2)}) collective-permute-start(bf16[2,256,512]{2,1,0:T(8,128)(2,1)S(1)} %fusion.10), channel_id=1, source_target_pairs={{2,0},{3,1},{4,2},{5,3},{6,4},{7,5},{8,6},{9,7},{10,8},{11,9},{12,... | collective-permute-start | bytes 1572872 | tf_op jit(solution)/shard_map/ppermute | solution.py:100
  124.8 22.1 %collective-permute-start.11 = (bf16[2,256,512]{2,1,0:T(8,128)(2,1)S(1)}, bf16[2,256,512]{2,1,0:T(8,128)(2,1)S(1)}, u32[]{:S(2)}, u32[]{:S(2)}) collective-permute-start(bf16[2,256,512]{2,1,0:T(8,128)(2,1)S(1)} %fusion.8), channel_id=1, source_target_pairs={{2,0},{3,1},{4,2},{5,3},{6,4},{7,5},{8,6},{9,7},{10,8},{11,9},{12,... | collective-permute-start | bytes 1572872 | tf_op jit(solution)/shard_map/ppermute | solution.py:100
  127.8 19.1 %copy-start.7 = (f32[2,256,512]{2,1,0:T(8,128)S(1)}, f32[2,256,512]{2,1,0:T(8,128)}, u32[]{:S(2)}) copy-start(f32[2,256,512]{2,1,0:T(8,128)} %get-tuple-element.13) | copy-start | bytes 3145732
  136.0 22.1 %collective-permute-start.14 = (bf16[2,256,512]{2,1,0:T(8,128)(2,1)S(1)}, bf16[2,256,512]{2,1,0:T(8,128)(2,1)S(1)}, u32[]{:S(2)}, u32[]{:S(2)}) collective-permute-start(bf16[2,256,512]{2,1,0:T(8,128)(2,1)S(1)} %fusion.5), channel_id=1, source_target_pairs={{2,0},{3,1},{4,2},{5,3},{6,4},{7,5},{8,6},{9,7},{10,8},{11,9},{12,... | collective-permute-start | bytes 1572872 | tf_op jit(solution)/shard_map/ppermute | solution.py:100
  146.9 11.2 %copy-start.8 = (f32[2,256,512]{2,1,0:T(8,128)S(1)}, f32[2,256,512]{2,1,0:T(8,128)}, u32[]{:S(2)}) copy-start(f32[2,256,512]{2,1,0:T(8,128)} %get-tuple-element.15) | copy-start | bytes 3145732
